TPU v7x, 32 devices: a whole 2x2x4 slice. The times are simulated.
32 devices in a mesh: ctx: 8 (over y, x, core), mp: 4 (over z).
Axes of the slice: x: 2, y: 2, z: 4, core: 2. Of those that a mesh axis runs over, the one named last changes fastest.
Arguments:
- cotangent: bfloat16 [1536, 8192], P('ctx', 'mp'), may hold values from -6 to 6
- out_weight: bfloat16 [8192, 8192], P('mp', 'ctx'), may hold values from -0.0625 to 0.0625
- query_act: bfloat16 [1536, 8192], P('ctx', 'mp'), may hold values from -6 to 6
- key_act: bfloat16 [1536, 8192], P('ctx', 'mp'), may hold values from -6 to 6
- value_act: bfloat16 [1536, 8192], P('ctx', 'mp'), may hold values from -6 to 6
- filters: float32 [512, 128], replicated, may hold values from -0.5 to 0.5
Outputs:
- grad_query: bfloat16 [1536, 8192], P('ctx', 'mp')
- grad_key: bfloat16 [1536, 8192], P('ctx', 'mp')
- grad_value: bfloat16 [1536, 8192], P('ctx', 'mp')
- grad_filters: float32 [512, 128], replicated
All inputs are finite; a program needn't handle non-finite values.
Results may differ from a plain program's by a relative error of at most 0.0051.
Values may be sent and summed in bfloat16 or wider, within the bound.
No kernel may reach another device: no remote copies, remote signals or barrier semaphores. Data moves between devices by JAX's collectives and lax.ppermute only.
A program may use at most 128 MiB of HBM per device.

v0:
```python
import jax
import jax.numpy as jnp
from jax import lax
from jax.sharding import PartitionSpec as P


def causal(widened, taps, rows, prev):

    def causal_step(shift, total):
        window = lax.dynamic_slice_in_dim(widened, (prev - shift).astype(jnp.int32), rows, 0)
        weight = lax.dynamic_slice_in_dim(taps, shift.astype(jnp.int32), 1, 0)
        return total + weight * window

    return lax.fori_loop(
        jnp.int32(0),
        jnp.int32(prev + 1),
        causal_step,
        jnp.zeros((rows, widened.shape[1]), widened.dtype),
    )


def anticausal(trailing, taps, rows, prev):

    def anticausal_step(shift, total):
        window = lax.dynamic_slice_in_dim(trailing, shift.astype(jnp.int32), rows, 0)
        weight = lax.dynamic_slice_in_dim(taps, shift.astype(jnp.int32), 1, 0)
        return total + weight * window

    return lax.fori_loop(
        jnp.int32(0),
        jnp.int32(prev + 1),
        anticausal_step,
        jnp.zeros((rows, trailing.shape[1]), trailing.dtype),
    )


def lagged(widened, gradient, prev):
    rows = gradient.shape[0]

    def one_lag(shift):
        window = lax.dynamic_slice_in_dim(widened, prev - shift, rows, 0)
        return jnp.sum(window * gradient, axis=0)

    return lax.map(one_lag, jnp.arange(prev + 1, dtype=jnp.int32))


def contract(left, right):
    return lax.dot_general(
        left, right, (((1,), (1,)), ((), ())), preferred_element_type=jnp.float32
    )


def group_table(first, count, per_group, groups):
    channel = first + jnp.arange(count)
    return (channel[None, :] // per_group == jnp.arange(groups)[:, None]).astype(jnp.float32)


def body(cotangent, out_weight, query_act, key_act, value_act, filters):
    tok_rows, chans = cotangent.shape
    groups, taps_len = filters.shape
    prev = taps_len - 1
    ctx_count = lax.axis_size("ctx")
    per_group = chans * lax.axis_size("mp") // groups
    panel = lax.all_gather(out_weight, "ctx", axis=1, tiled=True)
    grad_mixed = contract(lax.all_gather(cotangent, "mp", axis=1, tiled=True), panel)
    product = (key_act.astype(jnp.float32) * value_act.astype(jnp.float32)).astype(jnp.bfloat16)
    grad_conv = (grad_mixed * query_act.astype(jnp.float32)).astype(jnp.bfloat16)
    narrow = chans // ctx_count
    seq_product, seq_grad = (
        lax.all_to_all(product, "ctx", split_axis=1, concat_axis=0, tiled=True),
        lax.all_to_all(grad_conv, "ctx", split_axis=1, concat_axis=0, tiled=True),
    )
    onehot = group_table(
        lax.axis_index("mp") * chans + lax.axis_index("ctx") * narrow, narrow, per_group, groups
    )
    taps = jnp.dot(filters.T, onehot, precision=lax.Precision.HIGHEST)
    seq_rows = seq_grad.shape[0]
    grad_wide = seq_grad.astype(jnp.float32)
    widened = jnp.concatenate(
        [jnp.zeros((prev, narrow), jnp.float32), seq_product.astype(jnp.float32)], 0
    )
    trailing = jnp.concatenate([grad_wide, jnp.zeros((prev, narrow), jnp.float32)], 0)
    seq_mixed = causal(widened, taps, seq_rows, prev)
    seq_back = anticausal(trailing, taps, seq_rows, prev)
    corr = lagged(widened, grad_wide, prev)
    mixed, grad_product = (
        lax.all_to_all(seq_mixed, "ctx", split_axis=0, concat_axis=1, tiled=True),
        lax.all_to_all(seq_back, "ctx", split_axis=0, concat_axis=1, tiled=True),
    )
    grad_query = (grad_mixed * mixed).astype(jnp.bfloat16)
    grad_key = (grad_product * value_act.astype(jnp.float32)).astype(jnp.bfloat16)
    grad_value = (grad_product * key_act.astype(jnp.float32)).astype(jnp.bfloat16)
    partial_terms = jnp.dot(onehot, corr.T, precision=lax.Precision.HIGHEST)
    scale = (tok_rows * ctx_count * per_group) ** (-0.5)
    grad_filters = lax.psum(partial_terms, ("ctx", "mp")) * scale
    return (grad_query, grad_key, grad_value, grad_filters)


def solution(mesh):
    in_specs = (P("ctx", "mp"), P("mp", "ctx"), P("ctx", "mp"), P("ctx", "mp"), P("ctx", "mp"), P())
    out_specs = (P("ctx", "mp"), P("ctx", "mp"), P("ctx", "mp"), P())
    return jax.shard_map(body, mesh=mesh, in_specs=in_specs, out_specs=out_specs, check_vma=False)
```

profile of v0, /device:TPU:0, one launch (start us, length us, event | category | flops | bytes accessed | tf_op | source)
XLA Modules:
  0.0 1397.0 jit_solution(9679557478164837878)
XLA Ops:
  8.7 67.1 %all-gather.3.cloned.1.call-done = bf16[192,8192]{1,0:T(8,128)(2,1)} async-done(((bf16[192,2048]{1,0:T(8,128)(2,1)}), bf16[192,8192]{1,0:T(8,128)(2,1)}) %all-gather.3.cloned.1.call-update) | async-done | bytes 3145744 | tf_op jit(solution)/shard_map/all_gather | solution.py:65
  75.8 161.4 %all-gather.5.cloned.1.call-done = bf16[2048,8192]{1,0:T(8,128)(2,1)} async-done(((bf16[2048,1024]{1,0:T(8,128)(2,1)}), bf16[2048,8192]{1,0:T(8,128)(2,1)}) %all-gather.5.cloned.1.call-update) | async-done | bytes 33554448 | tf_op jit(solution)/shard_map/all_gather | solution.py:64
  237.2 18.0 %multiply_convert_fusion = (bf16[192,2048]{1,0:T(8,128)(2,1)S(1)}, f32[192,2048]{1,0:T(8,128)}) fusion(bf16[192,2048]{1,0:T(8,128)(2,1)S(1)} %copy-done.7, bf16[192,8192]{1,0:T(8,128)(2,1)} %all-gather.3.cloned.1.call-done, bf16[2048,8192]{1,0:T(8,128)(2,1)} %all-gather.5.cloned.1.call-done), kind=kOutput, calls=%fused_computation.11 | convolution fusion | flops 6443630592 | bytes 39845888 | tf_op jit(solution)/shard_map/dot_general | solution.py:48
  256.1 3.5 all-to-all-start.2
  260.5 11.8 all-to-all-done.2
  274.4 282.6 %while.38 = (s32[]{:T(128)}, f32[1536,256]{1,0:T(8,128)S(1)}, f32[128,256]{1,0:T(8,128)S(1)}, f32[1663,256]{1,0:T(8,128)}, s32[]{:T(128)}, /*index=5*/s32[]{:T(128)}) while((s32[]{:T(128)}, f32[1536,256]{1,0:T(8,128)S(1)}, f32[128,256]{1,0:T(8,128)S(1)}, f32[1663,256]{1,0:T(8,128)}, s32[]{:T(128)}, /*index=5*/s32[]{:T(128)}) %tuple.98), condition=%wide.region_3.4_spmd.clone, body=%wide.region_2.3_spmd.clone.sunk | while | flops 1179651 | bytes 4721759 | solution.py:29
  557.0 23.4 %all_to_all.64 = f32[8,192,256]{2,1,0:T(8,128)S(1)} all-to-all(f32[8,192,256]{2,1,0:T(8,128)S(1)} %bitcast.45), channel_id=1, replica_groups=mesh['ctx'=8,'mp'=4] {'ctx'}, dimensions={0} | all-to-all | bytes 3145728 | tf_op jit(solution)/shard_map/all_to_all | solution.py:88
  584.3 3.5 all-to-all-start
  587.9 12.5 all-to-all-done
  602.6 364.1 %while.37 = (s32[]{:T(128)}, f32[1536,256]{1,0:T(8,128)}, f32[128,256]{1,0:T(8,128)S(1)}, f32[1663,256]{1,0:T(8,128)S(1)}, s32[]{:T(128)}, /*index=5*/s32[]{:T(128)}, s32[]{:T(128)}, s32[]{:T(128)}) while((s32[]{:T(128)}, f32[1536,256]{1,0:T(8,128)}, f32[128,256]{1,0:T(8,128)S(1)}, f32[1663,256]{1,0:T(8,128)S(1)}, s32[]{:T(128)}, ...), condition=%wide.region_1.2_spmd.clone, body=%wide.region_0.1_spmd.clone.sunk | while | flops 1179655 | bytes 4721821 | solution.py:14
  607.0 2.9 select_add_fusion.4
  609.9 2.9 select_add_fusion.4
  618.6 2.9 select_add_fusion.4
  621.5 2.9 select_add_fusion.4
  646.9 2.9 select_add_fusion.4
  652.7 2.9 select_add_fusion.4
  655.6 2.9 select_add_fusion.4
  664.3 2.9 select_add_fusion.4
  667.2 2.9 select_add_fusion.4
  692.6 2.9 select_add_fusion.4
  698.4 2.9 select_add_fusion.4
  701.3 2.9 select_add_fusion.4
  710.0 2.9 select_add_fusion.4
  712.9 2.9 select_add_fusion.4
  738.3 2.9 select_add_fusion.4
  744.1 2.9 select_add_fusion.4
  747.0 2.9 select_add_fusion.4
  755.6 2.9 select_add_fusion.4
  758.5 2.9 select_add_fusion.4
  783.9 2.9 select_add_fusion.4
  789.7 2.9 select_add_fusion.4
  792.6 2.9 select_add_fusion.4
  801.3 2.9 select_add_fusion.4
  804.2 2.9 select_add_fusion.4
  829.6 2.9 select_add_fusion.4
  835.4 2.9 select_add_fusion.4
  838.3 2.9 select_add_fusion.4
  847.0 2.9 select_add_fusion.4
  849.9 2.9 select_add_fusion.4
  875.3 2.9 select_add_fusion.4
  881.1 2.9 select_add_fusion.4
  884.0 2.9 select_add_fusion.4
  892.7 2.9 select_add_fusion.4
  895.6 2.9 select_add_fusion.4
  921.0 2.9 select_add_fusion.4
  966.7 4.3 all-to-all-start.1
  971.0 287.3 %while.36 = (s32[]{:T(128)}, f32[128,256]{1,0:T(8,128)S(1)}, s32[128]{0:T(128)S(1)}, f32[1663,256]{1,0:T(8,128)S(1)}, f32[1536,256]{1,0:T(8,128)S(1)}, /*index=5*/s32[]{:T(128)}, s32[1]{0:T(128)}, s32[]{:T(128)}, s32[1]{0:T(128)}) while((s32[]{:T(128)}, f32[128,256]{1,0:T(8,128)S(1)}, s32[128]{0:T(128)S(1)}, f32[1663,256]{1,0:T(8,128)S(1)}, ...), condition=%wide.region_6.7_spmd, body=%wide.region_4.6_spmd.sunk | while | flops 786182 | bytes 3148967 | solution.py:44
  1259.5 126.4 %all-reduce.4.cloned.1.call-done = f32[512,128]{1,0:T(8,128)} async-done(((f32[512,128]{1,0:T(8,128)}), f32[512,128]{1,0:T(8,128)}) %all-reduce.4.cloned.1.call-update) | async-done | bytes 262160 | tf_op jit(solution)/shard_map/psum | solution.py:95
  (902 shorter events, 676.7 us)
Async XLA Ops:
  7.2 252.6 %copy-start = (f32[512,128]{1,0:T(8,128)S(1)}, f32[512,128]{1,0:T(8,128)}, u32[]{:S(2)}) copy-start(f32[512,128]{1,0:T(8,128)} %param.17) | copy-start | bytes 786436
  7.2 68.6 %all-gather.3.cloned.1.call-start = ((), (), s32[]{:S(2)}) async-start(), calls=%async_computation.4 | async-start | bytes 3932160 | tf_op jit(solution)/shard_map/all_gather | solution.py:65
  7.9 229.3 %copy-start.7 = (bf16[192,2048]{1,0:T(8,128)(2,1)S(1)}, bf16[192,2048]{1,0:T(8,128)(2,1)}, u32[]{:S(2)}) copy-start(bf16[192,2048]{1,0:T(8,128)(2,1)} %param.14) | copy-start | bytes 2359300
  7.9 229.3 %all-gather.5.cloned.1.call-start = ((), (), s32[]{:S(2)}) async-start(), calls=%async_computation.5 | async-start | bytes 37748736 | tf_op jit(solution)/shard_map/all_gather | solution.py:64
  256.1 16.1 %all-to-all-start.2 = ((bf16[192,8,256]{2,0,1:T(8,128)(2,1)}), bf16[192,8,256]{2,0,1:T(8,128)(2,1)S(1)}, u32[]{:S(2)}, u32[]{:S(2)}) async-start(bf16[192,8,256]{2,0,1:T(8,128)(2,1)} %bitcast.31), calls=%async_computation.2 | async-start | bytes 1572864 | tf_op jit(solution)/shard_map/all_to_all | solution.py:71
  272.4 2.0 copy-start.2
  580.4 1.1 copy-start.5
  580.4 1.4 copy-start.6
  584.3 16.1 %all-to-all-start = ((bf16[192,8,256]{2,0,1:T(8,128)(2,1)}), bf16[192,8,256]{2,0,1:T(8,128)(2,1)S(1)}, u32[]{:S(2)}, u32[]{:S(2)}) async-start(bf16[192,8,256]{2,0,1:T(8,128)(2,1)} %bitcast.32), calls=%async_computation | async-start | bytes 1572864 | tf_op jit(solution)/shard_map/all_to_all | solution.py:70
  600.4 0.9 copy-start.3
  966.7 420.9 %all-to-all-start.1 = ((f32[8,192,256]{2,1,0:T(8,128)}), f32[8,192,256]{2,1,0:T(8,128)}, u32[]{:S(2)}, u32[]{:S(2)}) async-start(f32[8,192,256]{2,1,0:T(8,128)} %bitcast.46), calls=%async_computation.1 | async-start | bytes 3145728 | tf_op jit(solution)/shard_map/all_to_all | solution.py:87
  970.9 414.9 %all-reduce.4.cloned.1.call-start = ((), (), s32[]{:S(2)}) async-start(), calls=%async_computation.6 | async-start | bytes 524288 | tf_op jit(solution)/shard_map/psum | solution.py:95
  1387.5 1.9 copy-start.4
  1389.2 1.3 copy-start.1
Sparse Core Ops, SparseCore 0:
  9.6 66.1 all-gather.2
  77.7 159.4 all-gather.4
  1259.6 126.2 all-reduce.3
where the time goes:
time: 1410 us; the launch traced here: 1400 us
  other arithmetic  685 us (49%)
  waiting for transfers between devices  381 us (27%)
  loops' own time  173 us (12%)
  local copies, waits for them, and re-layouts  89.3 us (6%)
  blocking collectives  23.4 us (2%)
  matrix products  19.7 us (1%)
    add x128, other arithmetic, causal_step(): return total + weight * window  363 us
    add x128, other arithmetic, anticausal_step(): return total + weight * window  278 us
    another operation x1, loops' own time, lagged(): return lax.map(one_lag, jnp.arange(prev + 1, dtype=jnp.int32))  169 us
    all_gather x1, waiting for transfers between devices, body(): panel = lax.all_gather(out_weight, 'ctx', axis=1, tiled=True)  161 us
    psum x1, waiting for transfers between devices, body(): grad_filters = lax.psum(partial_terms, ('ctx', 'mp')) * scale  126 us
    dynamic_slice x128, local copies, waits for them, and re-layouts, lagged(): return lax.map(one_lag, jnp.arange(prev + 1, dtype=jnp.int32))  75 us
    all_gather x1, waiting for transfers between devices, body(): lax.all_gather(cotangent, 'mp', axis=1, tiled=True)  67.1 us
    reduce_sum x128, other arithmetic, one_lag(): return jnp.sum(window * gradient, axis=0)  38.9 us
  transfers between devices with their start and end apart: 6, of which 5 were waited for; matrix products, arithmetic and copies ran while one was open for 9% of the time, Pallas kernels for 0%

commit v1 on v0

--- a/solution.py
+++ b/solution.py
@@ -1,7 +1,15 @@
+import functools
 import jax
 import jax.numpy as jnp
 from jax import lax
 from jax.sharding import PartitionSpec as P
+
+
+def see_desk(in_array, comm_axis):
+    return lax.all_gather(in_array, comm_axis).sum(axis=0)
+
+
+_push_racks = functools.partial(see_desk, comm_axis=("ctx", "mp"))
 
 
 def causal(widened, taps, rows, prev):
@@ -92,7 +100,7 @@
     grad_value = (grad_product * key_act.astype(jnp.float32)).astype(jnp.bfloat16)
     partial_terms = jnp.dot(onehot, corr.T, precision=lax.Precision.HIGHEST)
     scale = (tok_rows * ctx_count * per_group) ** (-0.5)
-    grad_filters = lax.psum(partial_terms, ("ctx", "mp")) * scale
+    grad_filters = _push_racks(partial_terms) * scale
     return (grad_query, grad_key, grad_value, grad_filters)
 
 

time: 1410 us -> 1320 us (0.936)
  waiting for transfers between devices: 381 us -> 254 us
  blocking collectives: 23.4 us -> 47.9 us
  other arithmetic: 685 us -> 701 us
    psum x1 -> x0, waiting for transfers between devices: 126 us -> none  [body(): grad_filters = lax.psum(partial_terms, ('ctx', 'mp')) * scale]
    all_to_all x0 -> x1, blocking collectives: none -> 24.5 us  [body(): lax.all_to_all(seq_mixed, 'ctx', split_axis=0, concat_axis=1, tiled=True)]
  transfers between devices with their start and end apart: 6 -> 5, of which waited for: 5 -> 4; matrix products, arithmetic and copies ran while one was open for 9% -> 29% of each run, Pallas kernels for 0% -> 0%
where the time goes in v1:
time: 1320 us; the launch traced here: 1310 us
  other arithmetic  701 us (53%)
  waiting for transfers between devices  254 us (19%)
  loops' own time  173 us (13%)
  local copies, waits for them, and re-layouts  88.1 us (7%)
  blocking collectives  47.9 us (4%)
  matrix products  19.7 us (1%)
  between operations  13.9 us (1%)
    add x128, other arithmetic, causal_step(): return total + weight * window  375 us
    add x128, other arithmetic, anticausal_step(): return total + weight * window  278 us
    another operation x1, loops' own time, lagged(): return lax.map(one_lag, jnp.arange(prev + 1, dtype=jnp.int32))  169 us
    all_gather x1, waiting for transfers between devices, body(): panel = lax.all_gather(out_weight, 'ctx', axis=1, tiled=True)  161 us
    dynamic_slice x128, local copies, waits for them, and re-layouts, lagged(): return lax.map(one_lag, jnp.arange(prev + 1, dtype=jnp.int32))  75 us
    all_gather x1, waiting for transfers between devices, body(): lax.all_gather(cotangent, 'mp', axis=1, tiled=True)  67.1 us
    reduce_sum x128, other arithmetic, one_lag(): return jnp.sum(window * gradient, axis=0)  38.9 us
  transfers between devices with their start and end apart: 5, of which 4 were waited for; matrix products, arithmetic and copies ran while one was open for 29% of the time, Pallas kernels for 0%

profile of v1, /device:TPU:0, one launch (start us, length us, event | category | flops | bytes accessed | tf_op | source)
XLA Modules:
  0.0 1305.7 jit_solution(8903504853123754538)
XLA Ops:
  8.7 67.1 %all-gather.5.cloned.1.call-done = bf16[192,8192]{1,0:T(8,128)(2,1)} async-done(((bf16[192,2048]{1,0:T(8,128)(2,1)}), bf16[192,8192]{1,0:T(8,128)(2,1)}) %all-gather.5.cloned.1.call-update) | async-done | bytes 3145744 | tf_op jit(solution)/shard_map/all_gather | solution.py:73
  75.8 161.4 %all-gather.7.cloned.1.call-done = bf16[2048,8192]{1,0:T(8,128)(2,1)} async-done(((bf16[2048,1024]{1,0:T(8,128)(2,1)}), bf16[2048,8192]{1,0:T(8,128)(2,1)}) %all-gather.7.cloned.1.call-update) | async-done | bytes 33554448 | tf_op jit(solution)/shard_map/all_gather | solution.py:72
  237.2 18.0 %multiply_convert_fusion = (bf16[192,2048]{1,0:T(8,128)(2,1)S(1)}, f32[192,2048]{1,0:T(8,128)}) fusion(bf16[192,2048]{1,0:T(8,128)(2,1)S(1)} %copy-done.6, bf16[192,8192]{1,0:T(8,128)(2,1)} %all-gather.5.cloned.1.call-done, bf16[2048,8192]{1,0:T(8,128)(2,1)} %all-gather.7.cloned.1.call-done), kind=kOutput, calls=%fused_computation.11 | convolution fusion | flops 6443630592 | bytes 39845888 | tf_op jit(solution)/shard_map/dot_general | solution.py:56
  256.1 4.2 all-to-all-start.2
  261.1 11.9 all-to-all-done.2
  275.6 282.6 %while.38 = (s32[]{:T(128)}, f32[1536,256]{1,0:T(8,128)S(1)}, f32[128,256]{1,0:T(8,128)S(1)}, f32[1663,256]{1,0:T(8,128)}, s32[]{:T(128)}, /*index=5*/s32[]{:T(128)}) while((s32[]{:T(128)}, f32[1536,256]{1,0:T(8,128)S(1)}, f32[128,256]{1,0:T(8,128)S(1)}, f32[1663,256]{1,0:T(8,128)}, s32[]{:T(128)}, /*index=5*/s32[]{:T(128)}) %tuple.81), condition=%wide.region_3.4_spmd.clone, body=%wide.region_2.3_spmd.clone.sunk | while | flops 1179651 | bytes 4721759 | solution.py:37
  558.1 23.4 %all_to_all.64 = f32[8,192,256]{2,1,0:T(8,128)S(1)} all-to-all(f32[8,192,256]{2,1,0:T(8,128)S(1)} %bitcast.47), channel_id=1, replica_groups=mesh['ctx'=8,'mp'=4] {'ctx'}, dimensions={0} | all-to-all | bytes 3145728 | tf_op jit(solution)/shard_map/all_to_all | solution.py:96
  585.5 3.5 all-to-all-start
  589.1 12.5 all-to-all-done
  603.8 287.3 %while.36 = (s32[]{:T(128)}, f32[128,256]{1,0:T(8,128)S(1)}, s32[128]{0:T(128)S(1)}, f32[1663,256]{1,0:T(8,128)S(1)}, f32[1536,256]{1,0:T(8,128)S(1)}, /*index=5*/s32[]{:T(128)}, s32[1]{0:T(128)}, s32[]{:T(128)}, s32[1]{0:T(128)}) while((s32[]{:T(128)}, f32[128,256]{1,0:T(8,128)S(1)}, s32[128]{0:T(128)S(1)}, f32[1663,256]{1,0:T(8,128)S(1)}, ...), condition=%wide.region_6.7_spmd, body=%wide.region_4.6_spmd.sunk | while | flops 786182 | bytes 3148967 | solution.py:52
  892.2 375.4 %while.37 = (s32[]{:T(128)}, f32[1536,256]{1,0:T(8,128)}, f32[128,256]{1,0:T(8,128)S(1)}, f32[1663,256]{1,0:T(8,128)S(1)}, s32[]{:T(128)}, /*index=5*/s32[]{:T(128)}, s32[]{:T(128)}, s32[]{:T(128)}) while((s32[]{:T(128)}, f32[1536,256]{1,0:T(8,128)}, f32[128,256]{1,0:T(8,128)S(1)}, f32[1663,256]{1,0:T(8,128)S(1)}, s32[]{:T(128)}, ...), condition=%wide.region_1.2_spmd.clone, body=%wide.region_0.1_spmd.clone.sunk | while | flops 1179655 | bytes 4721821 | solution.py:22
  893.8 3.0 select_add_fusion.4
  896.8 3.0 select_add_fusion.4
  899.8 3.0 select_add_fusion.4
  905.8 3.0 select_add_fusion.4
  908.8 3.0 select_add_fusion.4
  937.9 3.2 select_add_fusion.4
  944.1 3.0 select_add_fusion.4
  950.1 3.0 select_add_fusion.4
  953.1 3.0 select_add_fusion.4
  956.1 3.0 select_add_fusion.4
  959.1 3.0 select_add_fusion.4
  965.0 3.0 select_add_fusion.4
  985.4 3.0 select_add_fusion.4
  991.4 3.0 select_add_fusion.4
  997.4 3.0 select_add_fusion.4
  1006.3 3.0 select_add_fusion.4
  1035.4 3.0 select_add_fusion.4
  1041.4 3.0 select_add_fusion.4
  1047.4 3.0 select_add_fusion.4
  1050.4 3.0 select_add_fusion.4
  1079.5 3.0 select_add_fusion.4
  1085.5 3.0 select_add_fusion.4
  1091.4 3.0 select_add_fusion.4
  1100.4 3.0 select_add_fusion.4
  1129.5 3.0 select_add_fusion.4
  1135.5 3.0 select_add_fusion.4
  1141.5 3.0 select_add_fusion.4
  1179.5 3.0 select_add_fusion.4
  1185.5 3.0 select_add_fusion.4
  1191.5 3.0 select_add_fusion.4
  1194.5 3.0 select_add_fusion.4
  1220.6 3.0 select_add_fusion.4
  1223.6 3.0 select_add_fusion.4
  1229.6 3.0 select_add_fusion.4
  1235.5 3.0 select_add_fusion.4
  1267.6 24.5 %all_to_all.65 = f32[8,192,256]{2,1,0:T(8,128)S(1)} all-to-all(f32[8,192,256]{2,1,0:T(8,128)} %bitcast.46), channel_id=1, replica_groups=mesh['ctx'=8,'mp'=4] {'ctx'}, dimensions={0} | all-to-all | bytes 3145728 | tf_op jit(solution)/shard_map/all_to_all | solution.py:95
  1294.6 3.8 reduce_sum.21
  (900 shorter events, 683.7 us)
Async XLA Ops:
  7.2 253.2 %copy-start = (f32[512,128]{1,0:T(8,128)S(1)}, f32[512,128]{1,0:T(8,128)}, u32[]{:S(2)}) copy-start(f32[512,128]{1,0:T(8,128)} %param.17) | copy-start | bytes 786436
  7.2 68.6 %all-gather.5.cloned.1.call-start = ((), (), s32[]{:S(2)}) async-start(), calls=%async_computation.4 | async-start | bytes 3932160 | tf_op jit(solution)/shard_map/all_gather | solution.py:73
  7.9 229.3 %copy-start.6 = (bf16[192,2048]{1,0:T(8,128)(2,1)S(1)}, bf16[192,2048]{1,0:T(8,128)(2,1)}, u32[]{:S(2)}) copy-start(bf16[192,2048]{1,0:T(8,128)(2,1)} %param.14) | copy-start | bytes 2359300
  7.9 229.3 %all-gather.7.cloned.1.call-start = ((), (), s32[]{:S(2)}) async-start(), calls=%async_computation.5 | async-start | bytes 37748736 | tf_op jit(solution)/shard_map/all_gather | solution.py:72
  256.1 16.8 %all-to-all-start.2 = ((bf16[192,8,256]{2,0,1:T(8,128)(2,1)}), bf16[192,8,256]{2,0,1:T(8,128)(2,1)}, u32[]{:S(2)}, u32[]{:S(2)}) async-start(bf16[192,8,256]{2,0,1:T(8,128)(2,1)} %bitcast.32), calls=%async_computation.2 | async-start | bytes 1572864 | tf_op jit(solution)/shard_map/all_to_all | solution.py:79
  581.6 1.1 copy-start.4
  581.6 1.4 copy-start.5
  585.5 16.1 %all-to-all-start = ((bf16[192,8,256]{2,0,1:T(8,128)(2,1)}), bf16[192,8,256]{2,0,1:T(8,128)(2,1)S(1)}, u32[]{:S(2)}, u32[]{:S(2)}) async-start(bf16[192,8,256]{2,0,1:T(8,128)(2,1)} %bitcast.33), calls=%async_computation | async-start | bytes 1572864 | tf_op jit(solution)/shard_map/all_to_all | solution.py:78
  589.0 705.5 %all-gather.9.cloned.1.call-start = ((), (), s32[]{:S(2)}) async-start(), calls=%async_computation.6 | async-start | bytes 8650752 | tf_op jit(solution)/shard_map/all_gather | solution.py:9
  601.6 0.9 copy-start.2
  1292.1 1.4 copy-start.3
  1294.6 4.6 copy-start.1
Sparse Core Ops, SparseCore 0:
  9.6 66.1 all-gather.4
  77.7 159.4 all-gather.6
  892.3 76.4 all-gather.8
